TPU v7x, 128 devices: a whole 4x4x4 slice. The times are simulated.
128 devices in a mesh: req: 64 (over z, y, x_hi, core), tok: 2 (over x_lo).
Axes of the slice: x: 4 (x_hi: 2, x_lo: 2; x = x_hi * 2 + x_lo), y: 4, z: 4, core: 2. Of those that a mesh axis runs over, the one named last changes fastest.
Arguments:
- hidden_in: bfloat16 [128, 256, 2560], P('req', 'tok'), may hold values from -40 to 40
- cache_keys: bfloat16 [128, 4096, 320], P('req', None, 'tok'), may hold values from -100 to 100
- stored_cache_values: bfloat16 [128, 4096, 320], P('req', None, 'tok'), may hold values from -5 to 5
- cache_lengths: int32 [128], P('req'), may hold values from 0 to 16384, as said below
- live_slots: int32 [128], replicated, may hold values from 0 to 1, as said below
- attn_gain: float32 [2560], replicated, may hold values from 0.1 to 1.9
- w_query: bfloat16 [2560, 1280], P(None, 'tok'), may hold values from -0.125 to 0.125
- key_weight: bfloat16 [2560, 320], P(None, 'tok'), may hold values from -0.125 to 0.125
- value_weight: bfloat16 [2560, 320], P(None, 'tok'), may hold values from -0.125 to 0.125
- w_out: bfloat16 [1280, 2560], P('tok'), may hold values from -0.15625 to 0.15625
- mlp_gain: float32 [2560], replicated, may hold values from 0.1 to 1.9
- w_gate: bfloat16 [2560, 3584], P(None, 'tok'), may hold values from -0.125 to 0.125
- w_up: bfloat16 [2560, 3584], P(None, 'tok'), may hold values from -0.125 to 0.125
- w_down: bfloat16 [3584, 2560], P('tok'), may hold values from -0.09375 to 0.09375
Outputs:
- hidden_out: bfloat16 [128, 256, 2560], P('req', 'tok')
- new_keys: bfloat16 [128, 256, 320], P('req', None, 'tok')
- new_values: bfloat16 [128, 256, 320], P('req', None, 'tok')
Inputs may be any that keep to these rules, and one draw needn't show every extreme that they name: `live_slots`: exactly 64 of the 128 slots are live; the 2 slots of one index of req hold 0, 1 or 2 live requests, and some index holds two. `cache_lengths`: 0 for a slot that is not live; some live slot has exactly 16384.
All inputs are finite; a program needn't handle non-finite values.
Results may differ from a plain program's by a relative error of at most 0.0095.
Values may be sent and summed in bfloat16 or wider, within the bound.
No kernel may reach another device: no remote copies, remote signals or barrier semaphores. Data moves between devices by JAX's collectives and lax.ppermute only.
A program may use at most 192 MiB of HBM per device.

v0:
```python
import jax
import jax.numpy as jnp
from jax import lax
from jax.sharding import PartitionSpec as P

HEAD_DIM = 80


EPSILON = 1e-05
ROPE_BASE = 10000.0


def rms_norm(values, norm_gain):
    widened = values.astype(jnp.float32)
    mean_square = jnp.mean(widened * widened, axis=-1, keepdims=True)
    return widened * lax.rsqrt(mean_square + EPSILON) * norm_gain


def apply_rotary(values, token_positions):
    full_width = values.shape[-1]
    half_width = full_width // 2
    inverse = ROPE_BASE ** (-(jnp.arange(half_width, dtype=jnp.float32) * 2.0) / full_width)
    angles = token_positions.astype(jnp.float32)[..., None] * inverse
    cosine = jnp.cos(angles)[..., None, :]
    sine_part = jnp.sin(angles)[..., None, :]
    first_half = values[..., :half_width]
    second_half = values[..., half_width:]
    return jnp.concatenate(
        [
            first_half * cosine - second_half * sine_part,
            second_half * cosine + first_half * sine_part,
        ],
        axis=-1,
    )


def attend(
    query_rows, cached_keys, cached_values, recent_keys, recent_values, length, query_group_count
):
    row_total = query_rows.shape[0]
    recent_count = recent_keys.shape[0]
    window = cached_keys.shape[0]
    block_size = min(512, window)
    block_count = window // block_size
    scaling = query_rows.shape[1] ** (-0.5)
    query_pos = length + jnp.arange(row_total, dtype=jnp.int32) // query_group_count

    def cache_scores(block_index):
        key_block = lax.dynamic_slice_in_dim(cached_keys, block_index * block_size, block_size, 0)
        scores = (
            jnp.einsum("rd,kd->rk", query_rows, key_block, preferred_element_type=jnp.float32)
            * scaling
        )
        key_pos = (
            length - window + block_index * block_size + jnp.arange(block_size, dtype=jnp.int32)
        )
        visible = (key_pos[None, :] >= 0) & (query_pos[:, None] - key_pos[None, :] < window)
        return jnp.where(visible, scores, -jnp.inf)

    recent_pos = length + jnp.arange(recent_count, dtype=jnp.int32)
    recent_scores = (
        jnp.einsum("rd,kd->rk", query_rows, recent_keys, preferred_element_type=jnp.float32)
        * scaling
    )
    recent_visible = (recent_pos[None, :] <= query_pos[:, None]) & (
        query_pos[:, None] - recent_pos[None, :] < window
    )
    recent_scores = jnp.where(recent_visible, recent_scores, -jnp.inf)
    start_top = jnp.max(recent_scores, axis=1, keepdims=True)
    start_mass = jnp.sum(jnp.exp(recent_scores - start_top), axis=1, keepdims=True)
    first_block = jnp.maximum(window - length, 0) // block_size
    score_store = jnp.full((block_count, row_total, block_size), -jnp.inf, jnp.float32)

    def add_stats(block_index, carry):
        top, mass, stored = carry
        scores = cache_scores(block_index)
        stored = lax.dynamic_update_index_in_dim(stored, scores, block_index, 0)
        raised = jnp.maximum(top, jnp.max(scores, axis=1, keepdims=True))
        mass = mass * jnp.exp(top - raised) + jnp.sum(
            jnp.exp(scores - raised), axis=1, keepdims=True
        )
        return (raised, mass, stored)

    top, mass, score_store = lax.fori_loop(
        first_block, block_count, add_stats, (start_top, start_mass, score_store)
    )

    def weights(scores):
        return (jnp.exp(scores - top) / mass).astype(jnp.bfloat16)

    start_sum = jnp.dot(weights(recent_scores), recent_values, preferred_element_type=jnp.float32)

    def add_values(block_index, running):
        value_block = lax.dynamic_slice_in_dim(
            cached_values, block_index * block_size, block_size, 0
        )
        scores = lax.dynamic_index_in_dim(score_store, block_index, 0, keepdims=False)
        return running + jnp.dot(weights(scores), value_block, preferred_element_type=jnp.float32)

    return lax.fori_loop(first_block, block_count, add_values, start_sum)


def feed_forward(rows_in, mlp_gain, w_gate, w_up, w_down):
    normed_rows = rms_norm(rows_in, mlp_gain).astype(jnp.bfloat16)
    block_rows = lax.all_gather(normed_rows, "tok", axis=0, tiled=True)
    gate_part = jnp.dot(block_rows, w_gate, preferred_element_type=jnp.float32)
    up_part = jnp.dot(block_rows, w_up, preferred_element_type=jnp.float32)
    activated = (jax.nn.silu(gate_part) * up_part).astype(jnp.bfloat16)
    summed = lax.psum_scatter(
        jnp.dot(
            lax.slice_in_dim(activated, 0, rows_in.shape[0] * lax.axis_size("tok"), axis=0),
            w_down,
            preferred_element_type=jnp.float32,
        ).astype(jnp.bfloat16),
        "tok",
        scatter_dimension=0,
        tiled=True,
    ).astype(jnp.float32)
    return (rows_in.astype(jnp.float32) + summed).astype(jnp.bfloat16)


def local(
    hidden_in,
    cache_keys,
    stored_cache_values,
    cache_lengths,
    live_slots,
    attn_gain,
    w_query,
    key_weight,
    value_weight,
    w_out,
    mlp_gain,
    w_gate,
    w_up,
    w_down,
):
    slots, quarter, model_width = hidden_in.shape
    new_rows = quarter * lax.axis_size("tok")
    query_width = w_query.shape[1]
    key_width = key_weight.shape[1]
    query_heads = query_width // HEAD_DIM
    key_heads = key_width // HEAD_DIM
    query_group_count = query_heads // key_heads
    alive_slots = lax.dynamic_slice_in_dim(live_slots, lax.axis_index("req") * slots, slots)
    window_mask = alive_slots[:, None, None] > 0
    empty_value_rows = jnp.zeros((), jnp.bfloat16)
    normed = rms_norm(hidden_in, attn_gain).astype(jnp.bfloat16)
    block_rows = lax.all_gather(normed, "tok", axis=1, tiled=True)
    mixed_rows = jnp.concatenate(
        [
            jnp.einsum("srd,dh->srh", block_rows, matrix, preferred_element_type=jnp.float32)
            for matrix in (w_query, key_weight, value_weight)
        ],
        axis=2,
    )
    token_positions = cache_lengths[:, None] + jnp.arange(new_rows, dtype=jnp.int32)[None, :]
    queries = apply_rotary(
        mixed_rows[..., :query_width].reshape(slots, new_rows, query_heads, HEAD_DIM),
        token_positions,
    ).astype(jnp.bfloat16)
    incoming_keys = apply_rotary(
        mixed_rows[..., query_width : query_width + key_width].reshape(
            slots, new_rows, key_heads, HEAD_DIM
        ),
        token_positions,
    ).astype(jnp.bfloat16)
    incoming_values = (
        mixed_rows[..., query_width + key_width :]
        .astype(jnp.bfloat16)
        .reshape(slots, new_rows, key_heads, HEAD_DIM)
    )
    new_keys = jnp.where(
        window_mask, incoming_keys.reshape(slots, new_rows, key_width), empty_value_rows
    )
    new_values = jnp.where(
        window_mask, incoming_values.reshape(slots, new_rows, key_width), empty_value_rows
    )
    slot_results = []
    for slot_index in range(slots):
        head_results = []
        for current_head_index in range(key_heads):
            query_rows = queries[
                slot_index,
                :,
                current_head_index
                * query_group_count : (current_head_index + 1)
                * query_group_count,
                :,
            ].reshape(new_rows * query_group_count, HEAD_DIM)
            final_output = attend(
                query_rows,
                cache_keys[
                    slot_index,
                    :,
                    current_head_index * HEAD_DIM : (current_head_index + 1) * HEAD_DIM,
                ],
                stored_cache_values[
                    slot_index,
                    :,
                    current_head_index * HEAD_DIM : (current_head_index + 1) * HEAD_DIM,
                ],
                incoming_keys[slot_index, :, current_head_index, :],
                incoming_values[slot_index, :, current_head_index, :],
                cache_lengths[slot_index],
                query_group_count,
            )
            head_results.append(final_output.reshape(new_rows, query_group_count * HEAD_DIM))
        slot_results.append(jnp.concatenate(head_results, axis=1))
    attended = jnp.stack(slot_results, axis=0).astype(jnp.bfloat16)
    block_rows = attended
    projected = lax.psum_scatter(
        jnp.einsum("sth,hd->tsd", block_rows, w_out, preferred_element_type=jnp.float32).astype(
            jnp.bfloat16
        ),
        "tok",
        scatter_dimension=0,
        tiled=True,
    ).astype(jnp.float32)
    projected = jnp.transpose(projected, (1, 0, 2))
    residual = (hidden_in.astype(jnp.float32) + projected).astype(jnp.bfloat16)
    spread_rows = lax.all_to_all(residual, "req", split_axis=1, concat_axis=0, tiled=True)
    picked_index = jnp.nonzero(live_slots > 0, size=lax.axis_size("req"), fill_value=0)[0].astype(
        jnp.int32
    )
    picked = jnp.take(spread_rows, picked_index, axis=0)
    completed_output = feed_forward(
        picked.reshape(-1, model_width), mlp_gain, w_gate, w_up, w_down
    ).reshape(picked.shape)
    placed = jnp.zeros_like(spread_rows).at[picked_index].set(completed_output)
    hidden_out = lax.all_to_all(placed, "req", split_axis=0, concat_axis=1, tiled=True)
    return (hidden_out, new_keys, new_values)


def solution(mesh):
    return jax.shard_map(
        local,
        mesh=mesh,
        in_specs=(
            P("req", "tok", None),
            P("req", None, "tok"),
            P("req", None, "tok"),
            P("req"),
            P(),
            P(),
            P(None, "tok"),
            P(None, "tok"),
            P(None, "tok"),
            P("tok", None),
            P(),
            P(None, "tok"),
            P(None, "tok"),
            P("tok", None),
        ),
        out_specs=(P("req", "tok", None), P("req", None, "tok"), P("req", None, "tok")),
        check_vma=False,
    )
```

profile of v0, /device:TPU:1, one launch (start us, length us, event | category | flops | bytes accessed | tf_op | source)
XLA Modules:
  0.0 696.3 jit_solution(1556446365419780)
XLA Ops:
  14.8 3.2 fusion.113
  20.2 3.2 fusion.112
  43.5 12.5 %all-gather.3.cloned.1.call-done = bf16[2,256,2560]{2,1,0:T(8,128)(2,1)} async-done(((bf16[2,128,2560]{2,1,0:T(8,128)(2,1)}), bf16[2,256,2560]{2,1,0:T(8,128)(2,1)}) %all-gather.3.cloned.1.call-update) | async-done | bytes 2621456 | tf_op jit(solution)/shard_map/all_gather | solution.py:149
  55.9 4.6 fusion.62
  63.4 3.0 fusion.79
  68.1 7.9 %broadcast.455.clone.3 = f32[8,1024,512]{1,2,0:T(8,128)} broadcast(f32[]{:T(128)} %constant.371.clone.1), dimensions={} | broadcast | bytes 16777220 | tf_op jit(solution)/shard_map/broadcast.39
  76.0 3.7 broadcast_select_fusion.2
  88.0 7.9 %broadcast.455.clone.2 = f32[8,1024,512]{1,2,0:T(8,128)} broadcast(f32[]{:T(128)} %constant.371.clone.1), dimensions={} | broadcast | bytes 16777220 | tf_op jit(solution)/shard_map/broadcast.39
  105.3 7.9 %broadcast.455.clone.1 = f32[8,1024,512]{1,2,0:T(8,128)} broadcast(f32[]{:T(128)} %constant.371.clone.1), dimensions={} | broadcast | bytes 16777220 | tf_op jit(solution)/shard_map/broadcast.39
  122.6 7.9 %broadcast.455.clone = f32[8,1024,512]{1,2,0:T(8,128)} broadcast(f32[]{:T(128)} %constant.371.clone.1), dimensions={} | broadcast | bytes 16777220 | tf_op jit(solution)/shard_map/broadcast.39
  138.2 3.7 fusion.60
  141.9 373.5 %reduce-scatter.3.cloned.1.call-done = bf16[128,2,2560]{2,0,1:T(8,128)(2,1)} async-done(((bf16[256,2,2560]{2,0,1:T(8,128)(2,1)}), bf16[128,2,2560]{2,0,1:T(8,128)(2,1)}) %reduce-scatter.3.cloned.1.call-update) | async-done | bytes 1310736 | tf_op jit(solution)/shard_map/reduce_scatter | solution.py:212
  519.9 10.6 %all-to-all-start = ((bf16[2,128,2560]{2,0,1:T(2,128)(2,1)}), bf16[2,128,2560]{2,0,1:T(2,128)(2,1)}, u32[]{:S(2)}, u32[]{:S(2)}) async-start(bf16[2,128,2560]{2,0,1:T(2,128)(2,1)} %copy.106), calls=%async_computation.1 | async-start | bytes 2621440 | tf_op jit(solution)/shard_map/all_to_all | solution.py:222
  534.8 18.1 %all-to-all-done = bf16[2,128,2560]{2,0,1:T(2,128)(2,1)} async-done(((bf16[2,128,2560]{2,0,1:T(2,128)(2,1)}), bf16[2,128,2560]{2,0,1:T(2,128)(2,1)}, u32[]{:S(2)}, u32[]{:S(2)}) %all-to-all-start) | async-done | bytes 1310752 | tf_op jit(solution)/shard_map/all_to_all | solution.py:222
  552.9 3.4 copy.107
  556.4 4.0 gather_fusion
  560.4 2.7 gather.7
  565.3 2.9 fusion.74
  568.5 21.8 %all-gather.5.cloned.1.call-done = bf16[256,2560]{1,0:T(8,128)(2,1)} async-done(((bf16[128,2560]{1,0:T(8,128)(2,1)}), bf16[256,2560]{1,0:T(8,128)(2,1)}) %all-gather.5.cloned.1.call-update) | async-done | bytes 1310736 | tf_op jit(solution)/shard_map/all_gather | solution.py:105
  590.3 7.8 %fusion.119 = f32[256,1792]{1,0:T(8,128)} fusion(bf16[256,2560]{1,0:T(8,128)(2,1)} %all-gather.5.cloned.1.call-done, bf16[2560,1792]{1,0:T(8,128)(2,1)} %param.41), kind=kOutput, calls=%fused_computation.247 | convolution fusion | flops 2348810240 | bytes 12320768 | tf_op jit(solution)/shard_map/dot_general | solution.py:106
  598.1 13.7 %convolution_convert_fusion.1 = bf16[256,2560]{1,0:T(8,128)(2,1)} fusion(bf16[1792,2560]{1,0:T(8,128)(2,1)} %param.43, bf16[256,2560]{1,0:T(8,128)(2,1)} %all-gather.5.cloned.1.call-done, bf16[2560,1792]{1,0:T(8,128)(2,1)} %param.42, f32[256,1792]{1,0:T(8,128)} %fusion.119), kind=kOutput, calls=%fused_computation.116 | convolution fusion | flops 4701028352 | bytes 22806528 | tf_op jit(solution)/shard_map/dot_general | solution.py:110
  611.8 26.9 %reduce-scatter.5.cloned.1.call-done = bf16[128,2560]{1,0:T(8,128)(2,1)} async-done(((bf16[256,2560]{1,0:T(8,128)(2,1)}), bf16[128,2560]{1,0:T(8,128)(2,1)}) %reduce-scatter.5.cloned.1.call-update) | async-done | bytes 655376 | tf_op jit(solution)/shard_map/reduce_scatter | solution.py:109
  645.4 8.9 %scatter_fusion = bf16[128,2,2560]{2,1,0:T(2,128)(2,1)} fusion(bf16[128,2,2560]{2,1,0:T(2,128)(2,1)} %broadcast_in_dim.207, s32[64]{0:T(128)S(1)} %get-tuple-element.714, bf16[64,2,2560]{2,1,0:T(2,128)(2,1)} %reshape.295), kind=kCustom, calls=%fused_computation.2 | custom fusion | bytes 1966336 | tf_op jit(solution)/shard_map/scatter | solution.py:230
  654.4 33.0 %all_to_all.36 = bf16[128,2,2560]{2,1,0:T(2,128)(2,1)S(1)} all-to-all(bf16[128,2,2560]{2,1,0:T(2,128)(2,1)} %scatter_fusion), channel_id=1, replica_groups=mesh['req'=64,'tok'=2] {'req'}, dimensions={0} | all-to-all | bytes 2621440 | tf_op jit(solution)/shard_map/all_to_all | solution.py:231
  (133 shorter events, 86.4 us)
Async XLA Ops:
  7.2 131.0 %copy-start = (bf16[640,2560]{1,0:T(8,128)(2,1)S(1)}, bf16[640,2560]{1,0:T(8,128)(2,1)}, u32[]{:S(2)}) copy-start(bf16[640,2560]{1,0:T(8,128)(2,1)} %param.39) | copy-start | bytes 9830404
  7.2 48.8 %all-gather.3.cloned.1.call-start = ((), (), s32[]{:S(2)}) async-start(), calls=%async_computation.4 | async-start | bytes 3932160 | tf_op jit(solution)/shard_map/all_gather | solution.py:149
  7.2 1.9 copy-start.5
  9.1 2.3 copy-start.15
  11.2 504.2 %reduce-scatter.3.cloned.1.call-start = ((), (), s32[]{:S(2)}) async-start(), calls=%async_computation.5 | async-start | bytes 3932160 | tf_op jit(solution)/shard_map/reduce_scatter | solution.py:212
  34.6 4.5 copy-start.18
  40.4 26.1 %copy-start.23 = (s32[256]{0:T(256)}, s32[256]{0:T(256)S(1)}, u32[]{:S(2)}) copy-start(s32[256]{0:T(256)S(1)} %iota_add_fusion.4) | copy-start | bytes 3076
  42.3 24.1 %copy-start.16 = (s32[1024]{0:T(1024)}, s32[1024]{0:T(1024)S(1)}, u32[]{:S(2)}) copy-start(s32[1024]{0:T(1024)S(1)} %fusion.97) | copy-start | bytes 12292
  63.4 3.1 copy-start.11
  66.4 1.6 copy-start.13
  66.9 1.0 copy-start.7
  68.1 7.9 %copy-start.12 = (bf16[1,256,4,80]{3,2,1,0:T(4,128)(2,1)S(1)}, bf16[1,256,4,80]{3,2,1,0:T(4,128)(2,1)}, u32[]{:S(2)}) copy-start(bf16[1,256,4,80]{3,2,1,0:T(4,128)(2,1)} %copy.96) | copy-start | bytes 491524
  76.0 3.8 copy-start.8
  79.7 1.1 copy-start.20
  80.8 4.9 copy-start.17
  98.2 4.7 copy-start.21
  104.1 1.0 copy-start.10
  115.4 4.7 copy-start.22
  121.4 1.0 copy-start.6
  517.4 13.0 %copy-start.19 = (s32[128]{0:T(128)S(1)}, s32[128]{0:T(128)}, u32[]{:S(2)}) copy-start(s32[128]{0:T(128)} %param.34) | copy-start | bytes 1540
  519.9 33.1 %all-to-all-start = ((bf16[2,128,2560]{2,0,1:T(2,128)(2,1)}), bf16[2,128,2560]{2,0,1:T(2,128)(2,1)}, u32[]{:S(2)}, u32[]{:S(2)}) async-start(bf16[2,128,2560]{2,0,1:T(2,128)(2,1)} %copy.106), calls=%async_computation.1 | async-start | bytes 2621440 | tf_op jit(solution)/shard_map/all_to_all | solution.py:222
  530.4 59.9 %all-gather.5.cloned.1.call-start = ((), (), s32[]{:S(2)}) async-start(), calls=%async_computation.6 | async-start | bytes 1966080 | tf_op jit(solution)/shard_map/all_gather | solution.py:105
  556.4 8.9 %copy-start.14 = (f32[2560]{0:T(1024)S(1)}, f32[2560]{0:T(1024)}, u32[]{:S(2)}) copy-start(f32[2560]{0:T(1024)} %param.40) | copy-start | bytes 30724
  568.2 70.5 %reduce-scatter.5.cloned.1.call-start = ((), (), s32[]{:S(2)}) async-start(), calls=%async_computation.7 | async-start | bytes 1966080 | tf_op jit(solution)/shard_map/reduce_scatter | solution.py:109
  (1 other events, 1.0 us)
Sparse Core Ops, SparseCore 0:
  11.4 44.5 all-gather.2
  142.0 373.3 reduce-scatter.2
  568.4 21.8 all-gather.4
  611.9 26.7 reduce-scatter.4
where the time goes:
time: 708 us; the launch traced here: 696 us
  waiting for transfers between devices  453 us (64%)
  local copies, waits for them, and re-layouts  102 us (14%)
  matrix products  48.6 us (7%)
  blocking collectives  33 us (5%)
  other arithmetic  31.5 us (4%)
  between operations  17.2 us (2%)
  starting transfers between devices  10.9 us (2%)
    reduce_scatter x1, waiting for transfers between devices, local(): lax.psum_scatter(jnp.einsum('sth,hd->tsd', block_rows, w_out, preferred_e...  374 us
    another operation x9, local copies, waits for them, and re-layouts  35.9 us
    all_to_all x1, blocking collectives, local(): lax.all_to_all(placed, 'req', split_axis=0, concat_axis=1, tiled=True)  33 us
    reduce_scatter x1, waiting for transfers between devices, feed_forward(): lax.psum_scatter(jnp.dot(lax.slice_in_dim(activated, 0, rows_in.shape[0]...  26.9 us
    unnamed x49, local copies, waits for them, and re-layouts  23 us
    all_gather x1, waiting for transfers between devices, feed_forward(): block_rows = lax.all_gather(normed_rows, 'tok', axis=0, tiled=True)  21.8 us
    all_to_all x1, waiting for transfers between devices, local(): lax.all_to_all(residual, 'req', split_axis=1, concat_axis=0, tiled=True)  18.1 us
  transfers between devices with their start and end apart: 5, of which 5 were waited for; matrix products, arithmetic and copies ran while one was open for 5% of the time, Pallas kernels for 0%

commit v1 on v0

--- a/solution.py
+++ b/solution.py
@@ -1,6 +1,10 @@
+import functools
+
 import jax
 import jax.numpy as jnp
 from jax import lax
+from jax.experimental import pallas as pl
+from jax.experimental.pallas import tpu as pltpu
 from jax.sharding import PartitionSpec as P
 
 HEAD_DIM = 80
@@ -34,70 +38,84 @@
     )
 
 
-def attend(
-    query_rows, cached_keys, cached_values, recent_keys, recent_values, length, query_group_count
-):
-    row_total = query_rows.shape[0]
-    recent_count = recent_keys.shape[0]
-    window = cached_keys.shape[0]
-    block_size = min(512, window)
-    block_count = window // block_size
-    scaling = query_rows.shape[1] ** (-0.5)
-    query_pos = length + jnp.arange(row_total, dtype=jnp.int32) // query_group_count
-
-    def cache_scores(block_index):
-        key_block = lax.dynamic_slice_in_dim(cached_keys, block_index * block_size, block_size, 0)
-        scores = (
-            jnp.einsum("rd,kd->rk", query_rows, key_block, preferred_element_type=jnp.float32)
-            * scaling
+NEG = -jnp.inf
+KEY_BLOCK = 512
+
+
+def attention_kernel(len_ref, q_ref, kc_ref, vc_ref, kn_ref, vn_ref, o_ref, *, group, scaling):
+    slot = pl.program_id(0)
+    rows = q_ref.shape[1]
+    window = kc_ref.shape[1]
+    fresh = kn_ref.shape[1]
+    heads_rows = fresh * group
+    length = len_ref[slot]
+    q = q_ref[0]
+    row = pl.program_id(1) * rows + lax.broadcasted_iota(jnp.int32, (rows, 1), 0)
+    token = (row % heads_rows) // group
+    dims = (((1,), (1,)), ((), ()))
+    scores = lax.dot_general(q, kn_ref[0], dims, preferred_element_type=jnp.float32) * scaling
+    fresh_pos = lax.broadcasted_iota(jnp.int32, (1, fresh), 1)
+    scores = jnp.where(fresh_pos <= token, scores, NEG)
+    top = jnp.max(scores, axis=1, keepdims=True)
+    raised = jnp.exp(scores - top)
+    mass = jnp.sum(raised, axis=1, keepdims=True)
+    total = jnp.dot(raised.astype(jnp.bfloat16), vn_ref[0], preferred_element_type=jnp.float32)
+    lowest = window - length
+    first_block = jnp.maximum(lowest, 0) // KEY_BLOCK
+
+    def body(block, carry):
+        top, mass, total = carry
+        begin = pl.multiple_of(block * KEY_BLOCK, KEY_BLOCK)
+        keys = kc_ref[0, pl.ds(begin, KEY_BLOCK), :]
+        values = vc_ref[0, pl.ds(begin, KEY_BLOCK), :]
+        scores = lax.dot_general(q, keys, dims, preferred_element_type=jnp.float32) * scaling
+        key_pos = begin + lax.broadcasted_iota(jnp.int32, (1, KEY_BLOCK), 1)
+        visible = (key_pos >= lowest) & (key_pos > token)
+        scores = jnp.where(visible, scores, NEG)
+        raised_top = jnp.maximum(top, jnp.max(scores, axis=1, keepdims=True))
+        shrink = jnp.exp(top - raised_top)
+        raised = jnp.exp(scores - raised_top)
+        mass = mass * shrink + jnp.sum(raised, axis=1, keepdims=True)
+        total = total * shrink + jnp.dot(
+            raised.astype(jnp.bfloat16), values, preferred_element_type=jnp.float32
         )
-        key_pos = (
-            length - window + block_index * block_size + jnp.arange(block_size, dtype=jnp.int32)
-        )
-        visible = (key_pos[None, :] >= 0) & (query_pos[:, None] - key_pos[None, :] < window)
-        return jnp.where(visible, scores, -jnp.inf)
-
-    recent_pos = length + jnp.arange(recent_count, dtype=jnp.int32)
-    recent_scores = (
-        jnp.einsum("rd,kd->rk", query_rows, recent_keys, preferred_element_type=jnp.float32)
-        * scaling
-    )
-    recent_visible = (recent_pos[None, :] <= query_pos[:, None]) & (
-        query_pos[:, None] - recent_pos[None, :] < window
-    )
-    recent_scores = jnp.where(recent_visible, recent_scores, -jnp.inf)
-    start_top = jnp.max(recent_scores, axis=1, keepdims=True)
-    start_mass = jnp.sum(jnp.exp(recent_scores - start_top), axis=1, keepdims=True)
-    first_block = jnp.maximum(window - length, 0) // block_size
-    score_store = jnp.full((block_count, row_total, block_size), -jnp.inf, jnp.float32)
-
-    def add_stats(block_index, carry):
-        top, mass, stored = carry
-        scores = cache_scores(block_index)
-        stored = lax.dynamic_update_index_in_dim(stored, scores, block_index, 0)
-        raised = jnp.maximum(top, jnp.max(scores, axis=1, keepdims=True))
-        mass = mass * jnp.exp(top - raised) + jnp.sum(
-            jnp.exp(scores - raised), axis=1, keepdims=True
-        )
-        return (raised, mass, stored)
-
-    top, mass, score_store = lax.fori_loop(
-        first_block, block_count, add_stats, (start_top, start_mass, score_store)
-    )
-
-    def weights(scores):
-        return (jnp.exp(scores - top) / mass).astype(jnp.bfloat16)
-
-    start_sum = jnp.dot(weights(recent_scores), recent_values, preferred_element_type=jnp.float32)
-
-    def add_values(block_index, running):
-        value_block = lax.dynamic_slice_in_dim(
-            cached_values, block_index * block_size, block_size, 0
-        )
-        scores = lax.dynamic_index_in_dim(score_store, block_index, 0, keepdims=False)
-        return running + jnp.dot(weights(scores), value_block, preferred_element_type=jnp.float32)
-
-    return lax.fori_loop(first_block, block_count, add_values, start_sum)
+        return raised_top, mass, total
+
+    top, mass, total = lax.fori_loop(first_block, window // KEY_BLOCK, body, (top, mass, total))
+    o_ref[0] = (total / mass).astype(o_ref.dtype)
+
+
+def attend_all(padded_queries, cache_keys, cache_values, fresh_keys, fresh_values, lengths, group):
+    slots, total_rows, width = padded_queries.shape
+    window = cache_keys.shape[1]
+    fresh = fresh_keys.shape[1]
+    rows = 512
+    scaling = HEAD_DIM ** (-0.5)
+    kernel = functools.partial(attention_kernel, group=group, scaling=scaling)
+    flops = 2 * 2 * slots * total_rows * (window + fresh) * width
+    cost = pl.CostEstimate(
+        flops=flops,
+        transcendentals=slots * total_rows * (window + fresh),
+        bytes_accessed=2 * (2 * padded_queries.size + 2 * cache_keys.size + 2 * fresh_keys.size),
+    )
+    return pl.pallas_call(
+        kernel,
+        grid_spec=pltpu.PrefetchScalarGridSpec(
+            num_scalar_prefetch=1,
+            grid=(slots, total_rows // rows),
+            in_specs=[
+                pl.BlockSpec((1, rows, width), lambda s, r, n: (s, r, 0)),
+                pl.BlockSpec((1, window, width), lambda s, r, n: (s, 0, 0)),
+                pl.BlockSpec((1, window, width), lambda s, r, n: (s, 0, 0)),
+                pl.BlockSpec((1, fresh, width), lambda s, r, n: (s, 0, 0)),
+                pl.BlockSpec((1, fresh, width), lambda s, r, n: (s, 0, 0)),
+            ],
+            out_specs=pl.BlockSpec((1, rows, width), lambda s, r, n: (s, r, 0)),
+        ),
+        out_shape=jax.ShapeDtypeStruct((slots, total_rows, width), jnp.bfloat16),
+        compiler_params=pltpu.CompilerParams(dimension_semantics=("arbitrary", "arbitrary")),
+        cost_estimate=cost,
+    )(lengths, padded_queries, cache_keys, cache_values, fresh_keys, fresh_values)
 
 
 def feed_forward(rows_in, mlp_gain, w_gate, w_up, w_down):
@@ -176,38 +194,36 @@
     new_values = jnp.where(
         window_mask, incoming_values.reshape(slots, new_rows, key_width), empty_value_rows
     )
-    slot_results = []
-    for slot_index in range(slots):
-        head_results = []
-        for current_head_index in range(key_heads):
-            query_rows = queries[
-                slot_index,
-                :,
-                current_head_index
-                * query_group_count : (current_head_index + 1)
-                * query_group_count,
-                :,
-            ].reshape(new_rows * query_group_count, HEAD_DIM)
-            final_output = attend(
-                query_rows,
-                cache_keys[
-                    slot_index,
-                    :,
-                    current_head_index * HEAD_DIM : (current_head_index + 1) * HEAD_DIM,
-                ],
-                stored_cache_values[
-                    slot_index,
-                    :,
-                    current_head_index * HEAD_DIM : (current_head_index + 1) * HEAD_DIM,
-                ],
-                incoming_keys[slot_index, :, current_head_index, :],
-                incoming_values[slot_index, :, current_head_index, :],
-                cache_lengths[slot_index],
-                query_group_count,
+    padded = []
+    for current_head_index in range(key_heads):
+        head_queries = queries[
+            :, :, current_head_index * query_group_count : (current_head_index + 1) * query_group_count, :
+        ].reshape(slots, new_rows * query_group_count, HEAD_DIM)
+        padded.append(
+            jnp.pad(
+                head_queries,
+                ((0, 0), (0, 0), (current_head_index * HEAD_DIM, (key_heads - 1 - current_head_index) * HEAD_DIM)),
             )
-            head_results.append(final_output.reshape(new_rows, query_group_count * HEAD_DIM))
-        slot_results.append(jnp.concatenate(head_results, axis=1))
-    attended = jnp.stack(slot_results, axis=0).astype(jnp.bfloat16)
+        )
+    attended_rows = attend_all(
+        jnp.concatenate(padded, axis=1),
+        cache_keys,
+        stored_cache_values,
+        incoming_keys.reshape(slots, new_rows, key_width),
+        incoming_values.reshape(slots, new_rows, key_width),
+        cache_lengths,
+        query_group_count,
+    )
+    head_rows = new_rows * query_group_count
+    attended = jnp.concatenate(
+        [
+            attended_rows[
+                :, h * head_rows : (h + 1) * head_rows, h * HEAD_DIM : (h + 1) * HEAD_DIM
+            ].reshape(slots, new_rows, query_group_count * HEAD_DIM)
+            for h in range(key_heads)
+        ],
+        axis=2,
+    )
     block_rows = attended
     projected = lax.psum_scatter(
         jnp.einsum("sth,hd->tsd", block_rows, w_out, preferred_element_type=jnp.float32).astype(

time: 708 us -> 351 us (0.50); the launches traced: 696 us -> 348 us
  waiting for transfers between devices: 453 us -> 179 us
  local copies, waits for them, and re-layouts: 102 us -> 44.6 us
  Pallas kernels: 0 us -> 34.8 us
  blocking collectives: 33 us -> 0 us
  other arithmetic: 31.5 us -> 18.6 us
  matrix products: 48.6 us -> 36.3 us
  starting transfers between devices: 10.9 us -> 21.5 us
    reduce_scatter x1, waiting for transfers between devices: 374 us -> 57.8 us  [local(): lax.psum_scatter(jnp.einsum('sth,hd->tsd', block_rows, w_out, preferred_e...]
    another operation x9 -> x1, local copies, waits for them, and re-layouts: 35.9 us -> 0.1 us
    pallas_call x0 -> x1, Pallas kernels: none -> 34.8 us  [attend_all(): pl.pallas_call(kernel, grid_spec=pltpu.PrefetchScalarGridSpec(num_scalar_...]
    all_to_all x1 -> x0, blocking collectives: 33 us -> none  [local(): lax.all_to_all(placed, 'req', split_axis=0, concat_axis=1, tiled=True)]
    all_to_all x0 -> x1, waiting for transfers between devices: none -> 20.9 us  [local(): lax.all_to_all(placed, 'req', split_axis=0, concat_axis=1, tiled=True)]
    all_gather x1, waiting for transfers between devices: 12.5 us -> 32.9 us  [local(): block_rows = lax.all_gather(normed, 'tok', axis=1, tiled=True)]
    dot_general x8 -> x0, matrix products: 12 us -> none  [the longest x4 7.92 us: attend(): jnp.dot(weights(recent_scores), recent_values, preferred_element_type=jnp...]
    all_to_all x0 -> x1, starting transfers between devices: none -> 10.6 us  [local(): lax.all_to_all(placed, 'req', split_axis=0, concat_axis=1, tiled=True)]
  transfers between devices with their start and end apart: 5 -> 6, of which waited for: 5 -> 6; matrix products, arithmetic and copies ran while one was open for 5% -> 5% of each run, Pallas kernels for 0% -> 0%
where the time goes in v1:
time: 351 us; the launch traced here: 348 us
  waiting for transfers between devices  179 us (51%)
  local copies, waits for them, and re-layouts  44.6 us (13%)
  matrix products  36.3 us (10%)
  Pallas kernels  34.8 us (10%)
  starting transfers between devices  21.5 us (6%)
  other arithmetic  18.6 us (5%)
  between operations  14 us (4%)
    reduce_scatter x1, waiting for transfers between devices, local(): lax.psum_scatter(jnp.einsum('sth,hd->tsd', block_rows, w_out, preferred_e...  57.8 us
    pallas_call x1, Pallas kernels, attend_all(): pl.pallas_call(kernel, grid_spec=pltpu.PrefetchScalarGridSpec(num_scalar_...  34.8 us
    all_gather x1, waiting for transfers between devices, local(): block_rows = lax.all_gather(normed, 'tok', axis=1, tiled=True)  32.9 us
    reduce_scatter x1, waiting for transfers between devices, feed_forward(): lax.psum_scatter(jnp.dot(lax.slice_in_dim(activated, 0, rows_in.shape[0]...  26.9 us
    all_gather x1, waiting for transfers between devices, feed_forward(): block_rows = lax.all_gather(normed_rows, 'tok', axis=0, tiled=True)  21.8 us
    all_to_all x1, waiting for transfers between devices, local(): lax.all_to_all(placed, 'req', split_axis=0, concat_axis=1, tiled=True)  20.9 us
    all_to_all x1, waiting for transfers between devices, local(): lax.all_to_all(residual, 'req', split_axis=1, concat_axis=0, tiled=True)  18.2 us
    unnamed x27, local copies, waits for them, and re-layouts  14.1 us
  transfers between devices with their start and end apart: 6, of which 6 were waited for; matrix products, arithmetic and copies ran while one was open for 5% of the time, Pallas kernels for 0%

profile of v1, /device:TPU:1, one launch (start us, length us, event | category | flops | bytes accessed | tf_op | source)
XLA Modules:
  0.0 348.4 jit_solution(12134735190798015777)
XLA Ops:
  11.3 5.6 %copy.60.kc_ref = bf16[2,4096,160]{2,1,0:T(8,128)(2,1)} copy(bf16[2,4096,160]{1,2,0:T(8,128)(2,1)} %param.15) | data formatting | bytes 5242880 | tf_op args[1]
  16.9 5.6 %copy.61.vc_ref = bf16[2,4096,160]{2,1,0:T(8,128)(2,1)} copy(bf16[2,4096,160]{1,2,0:T(8,128)(2,1)} %param.16) | data formatting | bytes 5242880 | tf_op args[2]
  23.1 32.9 %all-gather.3.cloned.1.call-done = bf16[2,256,2560]{2,1,0:T(8,128)(2,1)} async-done(((bf16[2,128,2560]{2,1,0:T(8,128)(2,1)}), bf16[2,256,2560]{2,1,0:T(8,128)(2,1)}) %all-gather.3.cloned.1.call-update) | async-done | bytes 2621456 | tf_op jit(solution)/shard_map/all_gather | solution.py:167
  55.9 4.6 %fusion.4 = f32[2,256,640]{1,2,0:T(8,128)S(1)} fusion(bf16[2,256,2560]{2,1,0:T(8,128)(2,1)} %all-gather.3.cloned.1.call-done, bf16[2560,640]{1,0:T(8,128)(2,1)} %param.20), kind=kOutput, calls=%fused_computation.14 | convolution fusion | flops 1677721600 | bytes 7208960 | tf_op jit(solution)/shard_map/srd,dh->srh/dot_general | solution.py:170
  65.7 2.9 fusion.16
  69.6 3.3 fusion.11.q_ref
  72.9 2.7 broadcast_select_fusion.2
  75.6 34.8 %shard_map.157 = bf16[2,2048,160]{2,1,0:T(8,128)(2,1)} custom-call(s32[2]{0:T(128)} %len_ref.1, bf16[2,2048,160]{2,1,0:T(8,128)(2,1)} %fusion.11.q_ref, bf16[2,4096,160]{2,1,0:T(8,128)(2,1)} %copy.60.kc_ref, bf16[2,4096,160]{2,1,0:T(8,128)(2,1)} %copy.61.vc_ref, bf16[2,256,160]{2,1,0:T(8,128)(2,1)} %copy.62.kn_ref, bf16[2,256,160]{2,1,0:T(8,128)(2,1)} %get-tuple-element.29.vn_ref), custom_call_target="tpu_custom_call" | custom-call | flops 11408506880 | bytes 8192000 | tf_op jit(solution)/shard_map/pallas_call | solution.py:101
  110.4 2.5 fusion.34
  112.9 2.2 reshape.200
  115.1 2.2 reshape.201
  117.3 4.8 %fusion.2 = bf16[256,2,2560]{2,0,1:T(8,128)(2,1)} fusion(bf16[640,2560]{1,0:T(8,128)(2,1)S(1)} %copy-done, bf16[2,256,320]{2,1,0:T(8,128)(2,1)} %reshape.201, bf16[2,256,320]{2,1,0:T(8,128)(2,1)} %reshape.200), kind=kOutput, calls=%fused_computation.8 | convolution fusion | flops 1680343040 | bytes 6553600 | tf_op jit(solution)/shard_map/sth,hd->tsd/dot_general | solution.py:229
  122.2 57.8 %reduce-scatter.3.cloned.1.call-done = bf16[128,2,2560]{2,0,1:T(8,128)(2,1)} async-done(((bf16[256,2,2560]{2,0,1:T(8,128)(2,1)}), bf16[128,2,2560]{2,0,1:T(8,128)(2,1)}) %reduce-scatter.3.cloned.1.call-update) | async-done | bytes 1310736 | tf_op jit(solution)/shard_map/reduce_scatter | solution.py:228
  181.7 2.4 copy.63
  184.1 10.6 %all-to-all-start = ((bf16[2,128,2560]{2,0,1:T(2,128)(2,1)}), bf16[2,128,2560]{2,0,1:T(2,128)(2,1)S(1)}, u32[]{:S(2)}, u32[]{:S(2)}) async-start(bf16[2,128,2560]{2,0,1:T(2,128)(2,1)} %copy.63), calls=%async_computation.1 | async-start | bytes 2621440 | tf_op jit(solution)/shard_map/all_to_all | solution.py:238
  199.1 18.2 %all-to-all-done = bf16[2,128,2560]{2,0,1:T(2,128)(2,1)S(1)} async-done(((bf16[2,128,2560]{2,0,1:T(2,128)(2,1)}), bf16[2,128,2560]{2,0,1:T(2,128)(2,1)S(1)}, u32[]{:S(2)}, u32[]{:S(2)}) %all-to-all-start) | async-done | bytes 1310752 | tf_op jit(solution)/shard_map/all_to_all | solution.py:238
  223.7 21.8 %all-gather.5.cloned.1.call-done = bf16[256,2560]{1,0:T(8,128)(2,1)} async-done(((bf16[128,2560]{1,0:T(8,128)(2,1)}), bf16[256,2560]{1,0:T(8,128)(2,1)}) %all-gather.5.cloned.1.call-update) | async-done | bytes 1310736 | tf_op jit(solution)/shard_map/all_gather | solution.py:123
  245.5 7.9 %fusion.35 = f32[256,1792]{1,0:T(8,128)} fusion(bf16[256,2560]{1,0:T(8,128)(2,1)} %all-gather.5.cloned.1.call-done, bf16[2560,1792]{1,0:T(8,128)(2,1)} %param.25), kind=kOutput, calls=%fused_computation.83 | convolution fusion | flops 2348810240 | bytes 12320768 | tf_op jit(solution)/shard_map/dot_general | solution.py:124
  253.4 13.3 %convolution_convert_fusion.1 = bf16[256,2560]{1,0:T(8,128)(2,1)} fusion(bf16[1792,2560]{1,0:T(8,128)(2,1)} %param.27, bf16[256,2560]{1,0:T(8,128)(2,1)S(1)} %copy-done.9, bf16[2560,1792]{1,0:T(8,128)(2,1)} %param.26, f32[256,1792]{1,0:T(8,128)} %fusion.35), kind=kOutput, calls=%fused_computation.12 | convolution fusion | flops 4701028352 | bytes 22806528 | tf_op jit(solution)/shard_map/dot_general | solution.py:128
  266.8 26.9 %reduce-scatter.5.cloned.1.call-done = bf16[128,2560]{1,0:T(8,128)(2,1)} async-done(((bf16[256,2560]{1,0:T(8,128)(2,1)}), bf16[128,2560]{1,0:T(8,128)(2,1)}) %reduce-scatter.5.cloned.1.call-update) | async-done | bytes 655376 | tf_op jit(solution)/shard_map/reduce_scatter | solution.py:127
  297.0 8.1 %scatter_fusion = bf16[128,2,2560]{2,1,0:T(2,128)(2,1)} fusion(bf16[128,2,2560]{2,1,0:T(2,128)(2,1)} %broadcast_in_dim.66, s32[64]{0:T(128)S(1)} %get-tuple-element.16, bf16[64,2,2560]{2,1,0:T(2,128)(2,1)S(1)} %reshape.223), kind=kCustom, calls=%fused_computation.2 | custom fusion | bytes 1966336 | tf_op jit(solution)/shard_map/scatter | solution.py:246
  305.1 10.6 %all-to-all-start.1 = ((bf16[128,2,2560]{2,1,0:T(2,128)(2,1)}), bf16[128,2,2560]{2,1,0:T(2,128)(2,1)}, u32[]{:S(2)}, u32[]{:S(2)}) async-start(bf16[128,2,2560]{2,1,0:T(2,128)(2,1)} %scatter_fusion), calls=%async_computation.3 | async-start | bytes 2621440 | tf_op jit(solution)/shard_map/all_to_all | solution.py:247
  317.3 20.9 %all-to-all-done.1 = bf16[128,2,2560]{2,1,0:T(2,128)(2,1)} async-done(((bf16[128,2,2560]{2,1,0:T(2,128)(2,1)}), bf16[128,2,2560]{2,1,0:T(2,128)(2,1)}, u32[]{:S(2)}, u32[]{:S(2)}) %all-to-all-start.1) | async-done | bytes 1310752 | tf_op jit(solution)/shard_map/all_to_all | solution.py:247
  338.2 2.5 copy.65
  (72 shorter events, 29.3 us)
Async XLA Ops:
  7.2 110.2 %copy-start = (bf16[640,2560]{1,0:T(8,128)(2,1)S(1)}, bf16[640,2560]{1,0:T(8,128)(2,1)}, u32[]{:S(2)}) copy-start(bf16[640,2560]{1,0:T(8,128)(2,1)} %param.23) | copy-start | bytes 9830404
  7.2 48.8 %all-gather.3.cloned.1.call-start = ((), (), s32[]{:S(2)}) async-start(), calls=%async_computation.4 | async-start | bytes 3932160 | tf_op jit(solution)/shard_map/all_gather | solution.py:167
  7.2 1.9 copy-start.2
  11.2 168.8 %reduce-scatter.3.cloned.1.call-start = ((), (), s32[]{:S(2)}) async-start(), calls=%async_computation.5 | async-start | bytes 3932160 | tf_op jit(solution)/shard_map/reduce_scatter | solution.py:228
  16.9 5.6 %copy-start.10 = (s32[128]{0:T(128)S(1)}, s32[128]{0:T(128)}, u32[]{:S(2)}) copy-start(s32[128]{0:T(128)} %param.18) | copy-start | bytes 1540
  16.9 5.7 %copy-start.8 = (s32[2]{0:T(128)S(1)}, s32[2]{0:T(128)}, u32[]{:S(2)}) copy-start(s32[2]{0:T(128)} %len_ref.1) | copy-start | bytes 28
  69.6 3.3 copy-start.4
  69.6 3.3 copy-start.6
  122.2 57.9 %copy-start.3 = (bf16[2,128,2560]{2,1,0:T(8,128)(2,1)S(1)}, bf16[2,128,2560]{2,1,0:T(8,128)(2,1)}, u32[]{:S(2)}) copy-start(bf16[2,128,2560]{2,1,0:T(8,128)(2,1)} %param.14) | copy-start | bytes 3932164
  184.1 33.2 %all-to-all-start = ((bf16[2,128,2560]{2,0,1:T(2,128)(2,1)}), bf16[2,128,2560]{2,0,1:T(2,128)(2,1)S(1)}, u32[]{:S(2)}, u32[]{:S(2)}) async-start(bf16[2,128,2560]{2,0,1:T(2,128)(2,1)} %copy.63), calls=%async_computation.1 | async-start | bytes 2621440 | tf_op jit(solution)/shard_map/all_to_all | solution.py:238
  194.7 50.8 %all-gather.5.cloned.1.call-start = ((), (), s32[]{:S(2)}) async-start(), calls=%async_computation.6 | async-start | bytes 1966080 | tf_op jit(solution)/shard_map/all_gather | solution.py:123
  218.3 3.3 copy-start.7
  223.5 70.2 %reduce-scatter.5.cloned.1.call-start = ((), (), s32[]{:S(2)}) async-start(), calls=%async_computation.7 | async-start | bytes 1966080 | tf_op jit(solution)/shard_map/reduce_scatter | solution.py:127
  245.5 7.9 %copy-start.9 = (bf16[256,2560]{1,0:T(8,128)(2,1)S(1)}, bf16[256,2560]{1,0:T(8,128)(2,1)}, u32[]{:S(2)}) copy-start(bf16[256,2560]{1,0:T(8,128)(2,1)} %all-gather.5.cloned.1.call-done) | copy-start | bytes 3932164
  297.0 18.6 %copy-start.5 = (bf16[2,256,160]{2,1,0:T(8,128)(2,1)S(1)}, bf16[2,256,160]{2,1,0:T(8,128)(2,1)}, u32[]{:S(2)}) copy-start(bf16[2,256,160]{2,1,0:T(8,128)(2,1)} %get-tuple-element.28) | copy-start | bytes 491524
  305.1 33.1 %all-to-all-start.1 = ((bf16[128,2,2560]{2,1,0:T(2,128)(2,1)}), bf16[128,2,2560]{2,1,0:T(2,128)(2,1)}, u32[]{:S(2)}, u32[]{:S(2)}) async-start(bf16[128,2,2560]{2,1,0:T(2,128)(2,1)} %scatter_fusion), calls=%async_computation.3 | async-start | bytes 2621440 | tf_op jit(solution)/shard_map/all_to_all | solution.py:247
  338.2 3.7 %copy-start.1 = (bf16[640,2560]{1,0:T(8,128)(2,1)S(1)}, bf16[640,2560]{1,0:T(8,128)(2,1)}, u32[]{:S(2)}) copy-start(bf16[640,2560]{1,0:T(8,128)(2,1)} %param.23) | copy-start | bytes 9830404
Sparse Core Ops, SparseCore 0:
  11.4 44.5 all-gather.2
  122.3 57.6 reduce-scatter.2
  223.6 21.8 all-gather.4
  266.9 26.7 reduce-scatter.4

commit v2 on v1

--- a/solution.py
+++ b/solution.py
@@ -18,6 +18,25 @@
     widened = values.astype(jnp.float32)
     mean_square = jnp.mean(widened * widened, axis=-1, keepdims=True)
     return widened * lax.rsqrt(mean_square + EPSILON) * norm_gain
+
+
+def tok_gather(part, axis):
+    me = lax.axis_index("tok")
+    other = lax.ppermute(part, "tok", [(0, 1), (1, 0)])
+    first = jnp.where(me == 0, part, other)
+    second = jnp.where(me == 0, other, part)
+    return jnp.concatenate([first, second], axis=axis)
+
+
+def tok_reduce(whole, axis):
+    me = lax.axis_index("tok")
+    half = whole.shape[axis] // 2
+    low = lax.slice_in_dim(whole, 0, half, axis=axis)
+    high = lax.slice_in_dim(whole, half, 2 * half, axis=axis)
+    keep = jnp.where(me == 0, low, high)
+    send = jnp.where(me == 0, high, low).astype(jnp.bfloat16)
+    other = lax.ppermute(send, "tok", [(0, 1), (1, 0)])
+    return keep + other.astype(jnp.float32)
 
 
 def apply_rotary(values, token_positions):
@@ -120,20 +139,13 @@
 
 def feed_forward(rows_in, mlp_gain, w_gate, w_up, w_down):
     normed_rows = rms_norm(rows_in, mlp_gain).astype(jnp.bfloat16)
-    block_rows = lax.all_gather(normed_rows, "tok", axis=0, tiled=True)
+    block_rows = tok_gather(normed_rows, 0)
     gate_part = jnp.dot(block_rows, w_gate, preferred_element_type=jnp.float32)
     up_part = jnp.dot(block_rows, w_up, preferred_element_type=jnp.float32)
     activated = (jax.nn.silu(gate_part) * up_part).astype(jnp.bfloat16)
-    summed = lax.psum_scatter(
-        jnp.dot(
-            lax.slice_in_dim(activated, 0, rows_in.shape[0] * lax.axis_size("tok"), axis=0),
-            w_down,
-            preferred_element_type=jnp.float32,
-        ).astype(jnp.bfloat16),
-        "tok",
-        scatter_dimension=0,
-        tiled=True,
-    ).astype(jnp.float32)
+    summed = tok_reduce(
+        jnp.dot(activated, w_down, preferred_element_type=jnp.float32), 0
+    )
     return (rows_in.astype(jnp.float32) + summed).astype(jnp.bfloat16)
 
 
@@ -164,7 +176,7 @@
     window_mask = alive_slots[:, None, None] > 0
     empty_value_rows = jnp.zeros((), jnp.bfloat16)
     normed = rms_norm(hidden_in, attn_gain).astype(jnp.bfloat16)
-    block_rows = lax.all_gather(normed, "tok", axis=1, tiled=True)
+    block_rows = tok_gather(normed, 1)
     mixed_rows = jnp.concatenate(
         [
             jnp.einsum("srd,dh->srh", block_rows, matrix, preferred_element_type=jnp.float32)
@@ -225,15 +237,9 @@
         axis=2,
     )
     block_rows = attended
-    projected = lax.psum_scatter(
-        jnp.einsum("sth,hd->tsd", block_rows, w_out, preferred_element_type=jnp.float32).astype(
-            jnp.bfloat16
-        ),
-        "tok",
-        scatter_dimension=0,
-        tiled=True,
-    ).astype(jnp.float32)
-    projected = jnp.transpose(projected, (1, 0, 2))
+    projected = tok_reduce(
+        jnp.einsum("sth,hd->std", block_rows, w_out, preferred_element_type=jnp.float32), 1
+    )
     residual = (hidden_in.astype(jnp.float32) + projected).astype(jnp.bfloat16)
     spread_rows = lax.all_to_all(residual, "req", split_axis=1, concat_axis=0, tiled=True)
     picked_index = jnp.nonzero(live_slots > 0, size=lax.axis_size("req"), fill_value=0)[0].astype(

time: 351 us -> 285 us (0.81)
  waiting for transfers between devices: 179 us -> 101 us
  Pallas kernels: 34.8 us -> 58.7 us
  between operations: 14 us -> 0.95 us
  matrix products: 36.3 us -> 31 us
    reduce_scatter x2 -> x0, waiting for transfers between devices: 84.7 us -> none  [the longest x1 57.8 us: local(): lax.psum_scatter(jnp.einsum('sth,hd->tsd', block_rows, w_out, preferred_e...]
    ppermute x0 -> x4, waiting for transfers between devices: none -> 61.6 us  [the longest x2 32.1 us: tok_gather(): other = lax.ppermute(part, 'tok', [(0, 1), (1, 0)])]
    all_gather x2 -> x0, waiting for transfers between devices: 54.7 us -> none  [the longest x1 32.9 us: local(): block_rows = lax.all_gather(normed, 'tok', axis=1, tiled=True)]
    pallas_call x1, Pallas kernels: 34.8 us -> 58.7 us  [attend_all(): pl.pallas_call(kernel, grid_spec=pltpu.PrefetchScalarGridSpec(num_scalar_...]
    ppermute x0 -> x4, starting transfers between devices: none -> 4.89 us  [the longest x2 2.64 us: tok_gather(): other = lax.ppermute(part, 'tok', [(0, 1), (1, 0)])]
    unnamed x27 -> x39, local copies, waits for them, and re-layouts: 14.1 us -> 15.1 us
  transfers between devices with their start and end apart: 6 -> 6, of which waited for: 6 -> 6; matrix products, arithmetic and copies ran while one was open for 5% -> 6% of each run, Pallas kernels for 0% -> 0%
where the time goes in v2:
time: 285 us; the launch traced here: 283 us
  waiting for transfers between devices  101 us (35%)
  Pallas kernels  58.7 us (21%)
  local copies, waits for them, and re-layouts  47.4 us (17%)
  matrix products  31 us (11%)
  starting transfers between devices  23.5 us (8%)
  other arithmetic  20.7 us (7%)
    pallas_call x1, Pallas kernels, attend_all(): pl.pallas_call(kernel, grid_spec=pltpu.PrefetchScalarGridSpec(num_scalar_...  58.7 us
    ppermute x2, waiting for transfers between devices, tok_gather(): other = lax.ppermute(part, 'tok', [(0, 1), (1, 0)])  32.1 us
    ppermute x2, waiting for transfers between devices, tok_reduce(): other = lax.ppermute(send, 'tok', [(0, 1), (1, 0)])  29.5 us
    all_to_all x1, waiting for transfers between devices, local(): lax.all_to_all(placed, 'req', split_axis=0, concat_axis=1, tiled=True)  21 us
    all_to_all x1, waiting for transfers between devices, local(): lax.all_to_all(residual, 'req', split_axis=1, concat_axis=0, tiled=True)  18.2 us
    unnamed x39, local copies, waits for them, and re-layouts  15.1 us
    dot_general x1, matrix products, feed_forward(): jnp.dot(activated, w_down, preferred_element_type=jnp.float32)  12.7 us
    all_to_all x1, starting transfers between devices, local(): lax.all_to_all(residual, 'req', split_axis=1, concat_axis=0, tiled=True)  11.4 us
  transfers between devices with their start and end apart: 6, of which 6 were waited for; matrix products, arithmetic and copies ran while one was open for 6% of the time, Pallas kernels for 0%

profile of v2, /device:TPU:1, one launch (start us, length us, event | category | flops | bytes accessed | tf_op | source)
XLA Modules:
  0.0 283.0 jit_solution(2576876159472341759)
XLA Ops:
  6.7 5.5 %copy.60.kc_ref = bf16[2,4096,160]{2,1,0:T(8,128)(2,1)} copy(bf16[2,4096,160]{1,2,0:T(8,128)(2,1)} %param.15) | data formatting | bytes 5242880 | tf_op args[1]
  12.2 5.6 %copy.61.vc_ref = bf16[2,4096,160]{2,1,0:T(8,128)(2,1)} copy(bf16[2,4096,160]{1,2,0:T(8,128)(2,1)} %param.16) | data formatting | bytes 5242880 | tf_op args[2]
  18.4 16.6 %collective-permute-done = bf16[2,128,2560]{2,1,0:T(8,128)(2,1)} collective-permute-done((bf16[2,128,2560]{2,1,0:T(8,128)(2,1)}, bf16[2,128,2560]{2,1,0:T(8,128)(2,1)}, u32[]{:S(2)}, u32[]{:S(2)}) %collective-permute-start) | collective-permute-done | bytes 1310752 | tf_op jit(solution)/shard_map/ppermute | solution.py:25
  35.0 2.4 broadcast_select_fusion.2
  44.6 2.9 %fusion.19 = f32[2,256,160]{1,2,0:T(8,128)S(1)} fusion(bf16[2560,160]{0,1:T(8,128)(2,1)} %param.21, bf16[2,128,2560]{2,1,0:T(8,128)(2,1)} %copy-done.6, bf16[2,128,2560]{2,1,0:T(8,128)(2,1)} %copy-done.4), kind=kOutput, calls=%fused_computation.39 | convolution fusion | flops 424673280 | bytes 3768320 | tf_op jit(solution)/shard_map/srd,dh->srh/dot_general | solution.py:182
  48.5 3.3 %fusion.10.q_ref = bf16[2,2048,160]{2,1,0:T(8,128)(2,1)} fusion(bf16[2,1024,80]{2,1,0:T(8,128)(2,1)} %bitcast.37, bf16[2,1024,80]{2,1,0:T(8,128)(2,1)} %bitcast.36), kind=kLoop, calls=%fused_computation.20 | loop fusion | flops 5242880 | bytes 1966080 | tf_op jit(solution)/shard_map/concatenate | solution.py:221
  51.8 2.7 broadcast_select_fusion.6
  54.5 58.7 %shard_map.157 = bf16[2,2048,160]{2,1,0:T(8,128)(2,1)} custom-call(s32[2]{0:T(128)} %len_ref.1, bf16[2,2048,160]{2,1,0:T(8,128)(2,1)} %fusion.10.q_ref, bf16[2,4096,160]{2,1,0:T(8,128)(2,1)} %copy.60.kc_ref, bf16[2,4096,160]{2,1,0:T(8,128)(2,1)} %copy.61.vc_ref, bf16[2,256,160]{2,1,0:T(8,128)(2,1)} %copy.62.kn_ref, bf16[2,256,160]{2,1,0:T(8,128)(2,1)} %get-tuple-element.33.vn_ref), custom_call_target="tpu_custom_call" | custom-call | flops 11408506880 | bytes 8192000 | tf_op jit(solution)/shard_map/pallas_call | solution.py:120
  113.2 2.5 fusion.43
  115.7 2.2 reshape.200
  117.9 2.2 reshape.201
  120.1 3.3 %fusion.2 = f32[2,256,2560]{2,1,0:T(8,128)S(1)} fusion(bf16[640,2560]{1,0:T(8,128)(2,1)S(1)} %copy-done, bf16[2,256,320]{2,1,0:T(8,128)(2,1)} %reshape.201, bf16[2,256,320]{2,1,0:T(8,128)(2,1)} %reshape.200), kind=kOutput, calls=%fused_computation.10 | convolution fusion | flops 1679032320 | bytes 9175040 | tf_op jit(solution)/shard_map/sth,hd->std/dot_general | solution.py:241
  125.6 15.0 %collective-permute-done.1 = bf16[2,128,2560]{2,1,0:T(8,128)(2,1)S(1)} collective-permute-done((bf16[2,128,2560]{2,1,0:T(8,128)(2,1)S(1)}, bf16[2,128,2560]{2,1,0:T(8,128)(2,1)S(1)}, u32[]{:S(2)}, u32[]{:S(2)}) %collective-permute-start.1) | collective-permute-done | bytes 1310752 | tf_op jit(solution)/shard_map/ppermute | solution.py:38
  141.4 2.4 copy.63
  143.8 11.4 %all-to-all-start = ((bf16[2,128,2560]{2,0,1:T(2,128)(2,1)}), bf16[2,128,2560]{2,0,1:T(2,128)(2,1)S(1)}, u32[]{:S(2)}, u32[]{:S(2)}) async-start(bf16[2,128,2560]{2,0,1:T(2,128)(2,1)} %copy.63), calls=%async_computation | async-start | bytes 2621440 | tf_op jit(solution)/shard_map/all_to_all | solution.py:244
  159.6 18.2 %all-to-all-done = bf16[2,128,2560]{2,0,1:T(2,128)(2,1)S(1)} async-done(((bf16[2,128,2560]{2,0,1:T(2,128)(2,1)}), bf16[2,128,2560]{2,0,1:T(2,128)(2,1)S(1)}, u32[]{:S(2)}, u32[]{:S(2)}) %all-to-all-start) | async-done | bytes 1310752 | tf_op jit(solution)/shard_map/all_to_all | solution.py:244
  183.8 15.4 %collective-permute-done.2 = bf16[128,2560]{1,0:T(8,128)(2,1)S(1)} collective-permute-done((bf16[128,2560]{1,0:T(8,128)(2,1)S(1)}, bf16[128,2560]{1,0:T(8,128)(2,1)S(1)}, u32[]{:S(2)}, u32[]{:S(2)}) %collective-permute-start.2) | collective-permute-done | bytes 655392 | tf_op jit(solution)/shard_map/ppermute | solution.py:25
  201.3 7.4 %fusion.16 = f32[256,1792]{1,0:T(8,128)} fusion(bf16[2560,1792]{1,0:T(8,128)(2,1)} %param.26, bf16[128,2560]{1,0:T(8,128)(2,1)S(1)} %get-tuple-element.24, bf16[128,2560]{1,0:T(8,128)(2,1)S(1)} %get-tuple-element.23), kind=kOutput, calls=%fused_computation.36 | convolution fusion | flops 2351431680 | bytes 12320768 | tf_op jit(solution)/shard_map/dot_general | solution.py:144
  208.6 12.7 %fusion.14 = f32[256,2560]{1,0:T(8,128)S(1)} fusion(bf16[1792,2560]{1,0:T(8,128)(2,1)} %param.27, f32[256,1792]{1,0:T(8,128)} %fusion.16, bf16[2560,1792]{1,0:T(8,128)(2,1)} %param.25, bf16[128,2560]{1,0:T(8,128)(2,1)} %copy-done.9, bf16[128,2560]{1,0:T(8,128)(2,1)} %copy-done.8), kind=kOutput, calls=%fused_computation.34 | convolution fusion | flops 4702994432 | bytes 24117248 | tf_op jit(solution)/shard_map/dot_general | solution.py:147
  221.9 14.6 %collective-permute-done.3 = bf16[128,2560]{1,0:T(8,128)(2,1)S(1)} collective-permute-done((bf16[128,2560]{1,0:T(8,128)(2,1)S(1)}, bf16[128,2560]{1,0:T(8,128)(2,1)S(1)}, u32[]{:S(2)}, u32[]{:S(2)}) %collective-permute-start.3) | collective-permute-done | bytes 655392 | tf_op jit(solution)/shard_map/ppermute | solution.py:38
  241.4 8.1 %scatter_fusion = bf16[128,2,2560]{2,1,0:T(2,128)(2,1)} fusion(bf16[128,2,2560]{2,1,0:T(2,128)(2,1)} %broadcast_in_dim.66, s32[64]{0:T(128)S(1)} %get-tuple-element.16, bf16[64,2,2560]{2,1,0:T(2,128)(2,1)S(1)} %reshape.223), kind=kCustom, calls=%fused_computation.2 | custom fusion | bytes 1966336 | tf_op jit(solution)/shard_map/scatter | solution.py:252
  249.5 7.1 %all-to-all-start.1 = ((bf16[128,2,2560]{2,1,0:T(2,128)(2,1)}), bf16[128,2,2560]{2,1,0:T(2,128)(2,1)}, u32[]{:S(2)}, u32[]{:S(2)}) async-start(bf16[128,2,2560]{2,1,0:T(2,128)(2,1)} %scatter_fusion), calls=%async_computation.1 | async-start | bytes 2621440 | tf_op jit(solution)/shard_map/all_to_all | solution.py:253
  258.3 21.0 %all-to-all-done.1 = bf16[128,2,2560]{2,1,0:T(2,128)(2,1)} async-done(((bf16[128,2,2560]{2,1,0:T(2,128)(2,1)}), bf16[128,2,2560]{2,1,0:T(2,128)(2,1)}, u32[]{:S(2)}, u32[]{:S(2)}) %all-to-all-start.1) | async-done | bytes 1310752 | tf_op jit(solution)/shard_map/all_to_all | solution.py:253
  279.3 2.5 copy.65
  (84 shorter events, 38.0 us)
Async XLA Ops:
  0.6 119.5 %copy-start = (bf16[640,2560]{1,0:T(8,128)(2,1)S(1)}, bf16[640,2560]{1,0:T(8,128)(2,1)}, u32[]{:S(2)}) copy-start(bf16[640,2560]{1,0:T(8,128)(2,1)} %param.23) | copy-start | bytes 9830404
  0.6 1.9 copy-start.2
  4.6 30.4 %collective-permute-start = (bf16[2,128,2560]{2,1,0:T(8,128)(2,1)}, bf16[2,128,2560]{2,1,0:T(8,128)(2,1)}, u32[]{:S(2)}, u32[]{:S(2)}) collective-permute-start(bf16[2,128,2560]{2,1,0:T(8,128)(2,1)} %fusion.8), channel_id=1, source_target_pairs={{0,1},{1,0},{2,3},{3,2},{4,5},{5,4},{6,7},{7,6},{8,9},{9,8},{10,11... | collective-permute-start | bytes 3932168 | tf_op jit(solution)/shard_map/ppermute | solution.py:25
  12.2 5.6 %copy-start.16 = (s32[128]{0:T(128)S(1)}, s32[128]{0:T(128)}, u32[]{:S(2)}) copy-start(s32[128]{0:T(128)} %param.18) | copy-start | bytes 1540
  12.2 5.7 %copy-start.14 = (s32[2]{0:T(128)S(1)}, s32[2]{0:T(128)}, u32[]{:S(2)}) copy-start(s32[2]{0:T(128)} %len_ref.1) | copy-start | bytes 28
  12.2 22.8 %copy-start.13 = (f32[2560]{0:T(1024)S(1)}, f32[2560]{0:T(1024)}, u32[]{:S(2)}) copy-start(f32[2560]{0:T(1024)} %param.19) | copy-start | bytes 30724
  18.4 19.1 %copy-start.15 = (bf16[2560,640]{1,0:T(8,128)(2,1)S(1)}, bf16[2560,640]{1,0:T(8,128)(2,1)}, u32[]{:S(2)}) copy-start(bf16[2560,640]{1,0:T(8,128)(2,1)} %param.20) | copy-start | bytes 9830404
  37.5 1.9 copy-start.4
  37.5 1.9 copy-start.6
  48.5 3.3 %copy-start.5 = (bf16[2,128,2560]{2,1,0:T(8,128)(2,1)S(1)}, bf16[2,128,2560]{2,1,0:T(8,128)(2,1)}, u32[]{:S(2)}) copy-start(bf16[2,128,2560]{2,1,0:T(8,128)(2,1)} %copy-done.4) | copy-start | bytes 3932164
  48.5 3.3 %copy-start.7 = (bf16[2,128,2560]{2,1,0:T(8,128)(2,1)S(1)}, bf16[2,128,2560]{2,1,0:T(8,128)(2,1)}, u32[]{:S(2)}) copy-start(bf16[2,128,2560]{2,1,0:T(8,128)(2,1)} %copy-done.6) | copy-start | bytes 3932164
  48.5 3.3 %copy-start.11 = (bf16[2,256,160]{2,1,0:T(8,128)(2,1)S(1)}, bf16[2,256,160]{2,1,0:T(8,128)(2,1)}, u32[]{:S(2)}) copy-start(bf16[2,256,160]{2,1,0:T(8,128)(2,1)} %copy.62.kn_ref) | copy-start | bytes 491524
  123.5 17.1 %copy-start.3 = (bf16[2,128,2560]{2,1,0:T(8,128)(2,1)S(1)}, bf16[2,128,2560]{2,1,0:T(8,128)(2,1)}, u32[]{:S(2)}) copy-start(bf16[2,128,2560]{2,1,0:T(8,128)(2,1)} %param.14) | copy-start | bytes 3932164
  123.7 16.9 %collective-permute-start.1 = (bf16[2,128,2560]{2,1,0:T(8,128)(2,1)S(1)}, bf16[2,128,2560]{2,1,0:T(8,128)(2,1)S(1)}, u32[]{:S(2)}, u32[]{:S(2)}) collective-permute-start(bf16[2,128,2560]{2,1,0:T(8,128)(2,1)S(1)} %select_convert_fusion), channel_id=1, source_target_pairs={{0,1},{1,0},{2,3},{3,2},{4,5},{5,4},{6,7},{7,6},{8,9},{9,8},{10,11... | collective-permute-start | bytes 3932168 | tf_op jit(solution)/shard_map/ppermute | solution.py:38
  143.8 34.0 %all-to-all-start = ((bf16[2,128,2560]{2,0,1:T(2,128)(2,1)}), bf16[2,128,2560]{2,0,1:T(2,128)(2,1)S(1)}, u32[]{:S(2)}, u32[]{:S(2)}) async-start(bf16[2,128,2560]{2,0,1:T(2,128)(2,1)} %copy.63), calls=%async_computation | async-start | bytes 2621440 | tf_op jit(solution)/shard_map/all_to_all | solution.py:244
  178.9 3.3 %copy-start.12 = (f32[2560]{0:T(1024)S(1)}, f32[2560]{0:T(1024)}, u32[]{:S(2)}) copy-start(f32[2560]{0:T(1024)} %param.24) | copy-start | bytes 30724
  183.2 16.0 %collective-permute-start.2 = (bf16[128,2560]{1,0:T(8,128)(2,1)S(1)}, bf16[128,2560]{1,0:T(8,128)(2,1)S(1)}, u32[]{:S(2)}, u32[]{:S(2)}) collective-permute-start(bf16[128,2560]{1,0:T(8,128)(2,1)S(1)} %fusion.12), channel_id=1, source_target_pairs={{0,1},{1,0},{2,3},{3,2},{4,5},{5,4},{6,7},{7,6},{8,9},{9,8},{10,11... | collective-permute-start | bytes 1966088 | tf_op jit(solution)/shard_map/ppermute | solution.py:25
  200.2 0.8 copy-start.8
  200.2 1.0 copy-start.9
  221.5 14.9 %collective-permute-start.3 = (bf16[128,2560]{1,0:T(8,128)(2,1)S(1)}, bf16[128,2560]{1,0:T(8,128)(2,1)S(1)}, u32[]{:S(2)}, u32[]{:S(2)}) collective-permute-start(bf16[128,2560]{1,0:T(8,128)(2,1)S(1)} %select_convert_fusion.1), channel_id=1, source_target_pairs={{0,1},{1,0},{2,3},{3,2},{4,5},{5,4},{6,7},{7,6},{8,9},{9,8},{10,11... | collective-permute-start | bytes 1966088 | tf_op jit(solution)/shard_map/ppermute | solution.py:38
  241.4 15.2 %copy-start.10 = (bf16[2,256,160]{2,1,0:T(8,128)(2,1)S(1)}, bf16[2,256,160]{2,1,0:T(8,128)(2,1)}, u32[]{:S(2)}) copy-start(bf16[2,256,160]{2,1,0:T(8,128)(2,1)} %get-tuple-element.32) | copy-start | bytes 491524
  249.5 29.8 %all-to-all-start.1 = ((bf16[128,2,2560]{2,1,0:T(2,128)(2,1)}), bf16[128,2,2560]{2,1,0:T(2,128)(2,1)}, u32[]{:S(2)}, u32[]{:S(2)}) async-start(bf16[128,2,2560]{2,1,0:T(2,128)(2,1)} %scatter_fusion), calls=%async_computation.1 | async-start | bytes 2621440 | tf_op jit(solution)/shard_map/all_to_all | solution.py:253
  279.3 3.7 %copy-start.1 = (bf16[640,2560]{1,0:T(8,128)(2,1)S(1)}, bf16[640,2560]{1,0:T(8,128)(2,1)}, u32[]{:S(2)}) copy-start(bf16[640,2560]{1,0:T(8,128)(2,1)} %param.23) | copy-start | bytes 9830404
